TPU v7x, 256 devices: a whole 4x4x8 slice. The times are simulated.
256 devices in a mesh: ctx: 64 (over z, x, core), head: 4 (over y).
Axes of the slice: x: 4, y: 4, z: 8, core: 2. Of those that a mesh axis runs over, the one named last changes fastest.
Arguments:
- queries: bfloat16 [8192, 32, 128], P('ctx', 'head'), may hold values from -14 to 14
- keys: bfloat16 [8192, 32, 128], P('ctx', 'head'), may hold values from -14 to 14
- values: bfloat16 [8192, 32, 128], P('ctx', 'head'), may hold values from -6 to 6
- gain: float32 [32, 128], P('head'), may hold values from 0.1 to 1.9
- doc_lengths: int32 [64], replicated, may hold values from 1 to 2048, 8192 in all
- cotangent: bfloat16 [8192, 32, 128], P('ctx', 'head'), may hold values from -6 to 6
Outputs:
- mixed: bfloat16 [8192, 32, 128], P('ctx', 'head')
- query_grad: bfloat16 [8192, 32, 128], P('ctx', 'head')
- key_grad: bfloat16 [8192, 32, 128], P('ctx', 'head')
- value_grad: bfloat16 [8192, 32, 128], P('ctx', 'head')
All inputs are finite; a program needn't handle non-finite values.
Results may differ from a plain program's by a relative error of at most 0.0054.
Values may be sent and summed in bfloat16 or wider, within the bound.
No kernel may reach another device: no remote copies, remote signals or barrier semaphores. Data moves between devices by JAX's collectives and lax.ppermute only.
A program may use at most 128 MiB of HBM per device.

v0:
```python
import jax
import jax.numpy as jnp
from jax import lax
from jax.sharding import PartitionSpec as P

SPAN = 2
MAXDOC = 2048
neg_large = -1e30
norm_eps = 1e-06


def from_behind(x, axis, by):
    devices = lax.axis_size(axis)
    pairs = [(i, i + by) for i in range(devices) if 0 <= i + by < devices]
    return lax.ppermute(x, axis, pairs)


def send_state(x, axis, by):
    return from_behind(x.astype(jnp.bfloat16), axis, by).astype(jnp.float32)


def tile_state(keys_t, values_t, doc_lengths, start):
    tile = keys_t.shape[0]
    docs = doc_index(doc_lengths, start + jnp.arange(tile, dtype=jnp.int32))
    keep = (docs == docs[tile - 1])[:, None, None]
    return narrow("uhd,uhe->hde", jnp.where(keep, keys_t, jnp.zeros_like(keys_t)), values_t)


def fold_states(pieces, flags):
    total = pieces[0]
    for piece, flag in zip(pieces[1:], flags[1:]):
        total = piece + (1.0 - flag) * total
    return total


def front_flags(doc_lengths, spans, tile):
    low = jnp.stack([lo * tile - 1 for lo, hi in spans])
    high = jnp.stack([hi * tile + tile - 1 for lo, hi in spans])
    docs = doc_index(doc_lengths, jnp.concatenate([low, high]).astype(jnp.int32))
    count = len(spans)
    return (docs[:count] != docs[count:]).astype(jnp.float32)


def back_flags(doc_lengths, spans, tile):
    low = jnp.stack([lo * tile for lo, hi in spans])
    high = jnp.stack([hi * tile + tile for lo, hi in spans])
    docs = doc_index(doc_lengths, jnp.concatenate([low, high]).astype(jnp.int32))
    count = len(spans)
    return (docs[:count] != docs[count:]).astype(jnp.float32)


def wide(form, left, right):
    return jnp.einsum(form, left, right, precision=lax.Precision.HIGHEST)


def narrow(form, left, right):
    return jnp.einsum(form, left, right, preferred_element_type=jnp.float32)


def doc_index(doc_lengths, positions):
    starts = jnp.cumsum(doc_lengths) - doc_lengths
    return jnp.sum((starts[None, :] <= positions[:, None]).astype(jnp.int32), axis=1) - 1


def one_doc(doc_lengths, position):
    return doc_index(doc_lengths, jnp.reshape(position, (1,)))[0]


def masked_scores(query_block, key_block, mask, scale):
    raw = narrow("thd,uhd->htu", query_block, key_block) * scale
    return jnp.where(mask[None], raw, neg_large)


def key_terms(dscores, weights, query_block, grad_block, scale):
    key_part = narrow("htu,thd->uhd", dscores, query_block) * scale
    value_part = narrow("htu,thd->uhd", weights, grad_block)
    return (key_part, value_part)


def per_device(queries, keys, values, gain, doc_lengths, cotangent):
    tile, heads, width = queries.shape
    features = heads * lax.axis_size("head") * width
    scale = width ** (-0.5)
    base = lax.axis_index("ctx") * tile
    offsets = jnp.arange(tile, dtype=jnp.int32)
    own_pos = base + offsets
    own_doc = doc_index(doc_lengths, own_pos)
    prev_doc = one_doc(doc_lengths, base - 1)
    next_doc = one_doc(doc_lengths, base + tile)
    pair = jnp.stack([keys, values])
    arrived = [from_behind(pair, "ctx", shift) for shift in range(SPAN, 0, -1)]
    key_tiles = [piece[0] for piece in arrived] + [keys]
    value_tiles = [piece[1] for piece in arrived] + [values]
    masks = []
    for position in range(SPAN + 1):
        key_pos = base - (SPAN - position) * tile + offsets
        key_doc = doc_index(doc_lengths, key_pos)
        masks.append(
            (own_doc[:, None] == key_doc[None, :]) & (key_pos[None, :] <= own_pos[:, None])
        )
    score_list = [
        masked_scores(queries, key_tiles[position], masks[position], scale)
        for position in range(SPAN + 1)
    ]
    top = score_list[0].max(axis=-1)
    for position in range(1, SPAN + 1):
        top = jnp.maximum(top, score_list[position].max(axis=-1))
    total = jnp.zeros((heads, tile), jnp.float32)
    for position in range(SPAN + 1):
        total = total + jnp.sum(jnp.exp(score_list[position] - top[..., None]), axis=-1)
    log_total = top + jnp.log(total)
    prob_list = []
    weight_list = []
    soft_out = jnp.zeros((tile, heads, width), jnp.float32)
    for position in range(SPAN + 1):
        probs = jnp.exp(score_list[position] - log_total[..., None])
        weights = probs.astype(jnp.bfloat16)
        prob_list.append(probs)
        weight_list.append(weights)
        soft_out = soft_out + narrow("htu,uhd->thd", weights, value_tiles[position])
    same_tile = masks[SPAN].astype(jnp.float32)
    carried_prev = (own_doc == prev_doc).astype(jnp.float32)
    carried_next = (own_doc == next_doc).astype(jnp.float32)
    keep_first = (own_doc == own_doc[0])[:, None, None]
    query_wide = queries.astype(jnp.float32)
    attend = (narrow("thd,uhd->htu", queries, keys) * same_tile).astype(jnp.bfloat16)
    grad_wide = cotangent.astype(jnp.float32)
    row_dot = jnp.sum(grad_wide * soft_out, axis=-1).T
    query_soft = jnp.zeros((tile, heads, width), jnp.float32)
    dscore_list = []
    for position in range(SPAN + 1):
        dprobs = narrow("thd,uhd->htu", cotangent, value_tiles[position])
        dscores = (prob_list[position] * (dprobs - row_dot[..., None])).astype(jnp.bfloat16)
        query_soft = query_soft + narrow("htu,uhd->thd", dscores, key_tiles[position]) * scale
        dscore_list.append(dscores)
    parts = [
        key_terms(dscore_list[position], weight_list[position], queries, cotangent, scale)
        for position in range(SPAN + 1)
    ]
    outgoing = [
        jnp.stack(list(parts[SPAN - shift])).astype(jnp.bfloat16) for shift in range(1, SPAN + 1)
    ]
    place = lax.axis_index("ctx")
    need = min(-(-MAXDOC // tile), lax.axis_size("ctx"))
    near_states = [
        tile_state(
            key_tiles[position], value_tiles[position], doc_lengths, base - (SPAN - position) * tile
        )
        for position in range(SPAN)
    ]
    near_spans = [(place - SPAN + position, place - SPAN + position) for position in range(SPAN)]
    incoming = fold_states(near_states, front_flags(doc_lengths, near_spans, tile))
    covered = SPAN
    returned = None
    while covered < need:
        (flag,) = front_flags(doc_lengths, [(place - covered, place - 1)], tile)
        if 2 * covered >= need:
            incoming, outgoing = lax.optimization_barrier((incoming, outgoing))
            returned = [
                from_behind(outgoing[shift - 1], "ctx", -shift) for shift in range(1, SPAN + 1)
            ]
        incoming = incoming + (1.0 - flag) * send_state(incoming, "ctx", covered)
        covered *= 2
    linear_out = (
        narrow("htu,uhd->thd", attend, values)
        + wide("thd,hde->the", query_wide, incoming) * carried_prev[:, None, None]
    )
    weighted = cotangent.astype(jnp.float32) * gain[None]
    squares, projection = lax.psum(
        jnp.stack(
            [
                jnp.sum(linear_out * linear_out, axis=(1, 2)),
                jnp.sum(weighted * linear_out, axis=(1, 2)),
            ]
        ),
        "head",
    )
    inverse = lax.rsqrt(squares / features + norm_eps)
    mixed = (linear_out * inverse[:, None, None] * gain[None] + soft_out).astype(jnp.bfloat16)
    inner = (
        inverse[:, None, None] * weighted
        - linear_out * (inverse**3 * projection / features)[:, None, None]
    ).astype(jnp.bfloat16)
    inner_wide = inner.astype(jnp.float32)
    back = (narrow("thd,uhd->htu", inner, values) * same_tile).astype(jnp.bfloat16)
    query_linear = (
        narrow("htu,uhd->thd", back, keys)
        + wide("the,hde->thd", inner_wide, incoming) * carried_prev[:, None, None]
    )
    tile_sum = narrow(
        "thd,the->hde", jnp.where(keep_first, queries, jnp.zeros_like(queries)), inner
    )
    key_soft, value_soft = parts[SPAN]
    if returned is None:
        returned = [from_behind(outgoing[shift - 1], "ctx", -shift) for shift in range(1, SPAN + 1)]
    part = tile_sum
    covered = 1
    while 2 * covered < need:
        (flag,) = back_flags(doc_lengths, [(place, place + covered - 1)], tile)
        received = send_state(part, "ctx", -covered)
        if covered == 1:
            received, returned = lax.optimization_barrier((received, returned))
        part = part + (1.0 - flag) * received
        covered *= 2
    for moved in returned:
        key_soft = key_soft + moved[0].astype(jnp.float32)
        value_soft = value_soft + moved[1].astype(jnp.float32)
    later = send_state(part, "ctx", -1)
    if covered < need:
        (flag,) = back_flags(doc_lengths, [(place + 1, place + covered)], tile)
        later = later + (1.0 - flag) * send_state(part, "ctx", -1 - covered)
    key_linear = (
        narrow("htu,thd->uhd", back, queries)
        + wide("uhe,hde->uhd", values.astype(jnp.float32), later) * carried_next[:, None, None]
    )
    value_linear = (
        narrow("htu,the->uhe", attend, inner)
        + wide("uhd,hde->uhe", keys.astype(jnp.float32), later) * carried_next[:, None, None]
    )
    query_grad = (query_linear + query_soft).astype(jnp.bfloat16)
    key_grad = (key_linear + key_soft).astype(jnp.bfloat16)
    value_grad = (value_linear + value_soft).astype(jnp.bfloat16)
    return (mixed, query_grad, key_grad, value_grad)


def solution(mesh):
    placed = (
        P("ctx", "head", None),
        P("ctx", "head", None),
        P("ctx", "head", None),
        P("head", None),
        P(),
        P("ctx", "head", None),
    )
    return jax.shard_map(
        per_device,
        mesh=mesh,
        in_specs=placed,
        out_specs=(
            P("ctx", "head", None),
            P("ctx", "head", None),
            P("ctx", "head", None),
            P("ctx", "head", None),
        ),
        check_vma=False,
    )
```

profile of v0, /device:TPU:127, one launch (start us, length us, event | category | flops | bytes accessed | tf_op | source)
XLA Modules:
  0.0 135.6 jit_solution(5013973241469704528)
XLA Ops:
  0.6 1.1 copy_bitcast_fusion
  1.8 4.7 %collective-permute-start.1 = (bf16[2,128,8,128]{3,1,2,0:T(8,128)(2,1)S(1)}, bf16[2,128,8,128]{3,1,2,0:T(8,128)(2,1)S(1)}, u32[]{:S(2)}, u32[]{:S(2)}) collective-permute-start(bf16[2,128,8,128]{3,1,2,0:T(8,128)(2,1)S(1)} %pad_maximum_fusion), channel_id=1, source_target_pairs={{0,8},{4,12},{8,16},{12,20},{16,24},{20,28},{24,32},{28,36},{32,40... | collective-permute-start | bytes 1572872 | tf_op jit(solution)/shard_map/ppermute | solution.py:15
  6.5 4.0 %collective-permute-start = (bf16[2,128,8,128]{3,1,2,0:T(8,128)(2,1)S(1)}, bf16[2,128,8,128]{3,1,2,0:T(8,128)(2,1)S(1)}, u32[]{:S(2)}, u32[]{:S(2)}) collective-permute-start(bf16[2,128,8,128]{3,1,2,0:T(8,128)(2,1)S(1)} %pad_maximum_fusion), channel_id=1, source_target_pairs={{0,4},{4,8},{8,12},{12,16},{16,20},{20,24},{24,28},{28,32},{32,36}... | collective-permute-start | bytes 1572872 | tf_op jit(solution)/shard_map/ppermute | solution.py:15
  10.9 0.6 fusion.111
  13.9 0.6 fusion.126
  14.4 0.6 fusion.121
  15.1 0.6 fusion.122
  15.7 0.6 fusion.123
  16.3 0.6 slice.87
  16.9 0.6 slice.94
  17.7 1.3 broadcast_compare_fusion.1
  19.1 0.6 fusion.124
  19.7 0.7 fusion.125
  20.3 0.6 fusion.120
  20.9 0.6 slice.92
  32.3 0.6 copy-done
  33.4 0.7 copy-done.2
  35.1 3.1 %collective-permute-start.2 = (bf16[8,128,128]{2,1,0:T(8,128)(2,1)S(1)}, bf16[8,128,128]{2,1,0:T(8,128)(2,1)S(1)}, u32[]{:S(2)}, u32[]{:S(2)}) collective-permute-start(bf16[8,128,128]{2,1,0:T(8,128)(2,1)S(1)} %get-tuple-element.71), channel_id=1, source_target_pairs={{0,8},{4,12},{8,16},{12,20},{16,24},{20,28},{24,32},{28,36},{32,40... | collective-permute-start | bytes 786440 | tf_op jit(solution)/shard_map/ppermute | solution.py:15
  40.1 0.9 pad_maximum_fusion.2
  41.3 3.2 %collective-permute-done.2 = bf16[8,128,128]{2,1,0:T(8,128)(2,1)S(1)} collective-permute-done((bf16[8,128,128]{2,1,0:T(8,128)(2,1)S(1)}, bf16[8,128,128]{2,1,0:T(8,128)(2,1)S(1)}, u32[]{:S(2)}, u32[]{:S(2)}) %collective-permute-start.2) | collective-permute-done | bytes 262176 | tf_op jit(solution)/shard_map/ppermute | solution.py:15
  44.5 4.0 %collective-permute-start.3 = (bf16[8,128,128]{2,1,0:T(8,128)(2,1)S(1)}, bf16[8,128,128]{2,1,0:T(8,128)(2,1)S(1)}, u32[]{:S(2)}, u32[]{:S(2)}) collective-permute-start(bf16[8,128,128]{2,1,0:T(8,128)(2,1)S(1)} %fusion.54), channel_id=1, source_target_pairs={{0,16},{4,20},{8,24},{12,28},{16,32},{20,36},{24,40},{28,44},{32,4... | collective-permute-start | bytes 786440 | tf_op jit(solution)/shard_map/ppermute | solution.py:15
  48.6 0.9 pad_maximum_fusion.1
  49.8 6.0 %collective-permute-done.3 = bf16[8,128,128]{2,1,0:T(8,128)(2,1)S(1)} collective-permute-done((bf16[8,128,128]{2,1,0:T(8,128)(2,1)S(1)}, bf16[8,128,128]{2,1,0:T(8,128)(2,1)S(1)}, u32[]{:S(2)}, u32[]{:S(2)}) %collective-permute-start.3) | collective-permute-done | bytes 262176 | tf_op jit(solution)/shard_map/ppermute | solution.py:15
  55.9 2.6 %collective-permute-start.4 = (bf16[8,128,128]{2,1,0:T(8,128)(2,1)S(1)}, bf16[8,128,128]{2,1,0:T(8,128)(2,1)S(1)}, u32[]{:S(2)}, u32[]{:S(2)}) collective-permute-start(bf16[8,128,128]{2,1,0:T(8,128)(2,1)S(1)} %convert_element_type.228), channel_id=1, source_target_pairs={{0,32},{4,36},{8,40},{12,44},{16,48},{20,52},{24,56},{28,60},{32,6... | collective-permute-start | bytes 786440 | tf_op jit(solution)/shard_map/ppermute | solution.py:15
  58.5 1.1 fusion.14
  59.6 3.1 %collective-permute-start.6 = (bf16[2,128,8,128]{3,1,2,0:T(8,128)(2,1)}, bf16[2,128,8,128]{3,1,2,0:T(8,128)(2,1)}, u32[]{:S(2)}, u32[]{:S(2)}) collective-permute-start(bf16[2,128,8,128]{3,1,2,0:T(8,128)(2,1)} %pad_maximum_fusion.1), channel_id=1, source_target_pairs={{4,0},{8,4},{12,8},{16,12},{20,16},{24,20},{28,24},{32,28},{36,32}... | collective-permute-start | bytes 1572872 | tf_op jit(solution)/shard_map/ppermute | solution.py:15
  62.7 3.6 %collective-permute-start.7 = (bf16[2,128,8,128]{3,1,2,0:T(8,128)(2,1)}, bf16[2,128,8,128]{3,1,2,0:T(8,128)(2,1)}, u32[]{:S(2)}, u32[]{:S(2)}) collective-permute-start(bf16[2,128,8,128]{3,1,2,0:T(8,128)(2,1)} %pad_maximum_fusion.2), channel_id=1, source_target_pairs={{8,0},{12,4},{16,8},{20,12},{24,16},{28,20},{32,24},{36,28},{40,32... | collective-permute-start | bytes 1572872 | tf_op jit(solution)/shard_map/ppermute | solution.py:15
  66.4 0.5 fusion.30
  67.5 5.8 %psum.7 = f32[2,128]{1,0:T(2,128)S(1)} all-reduce(f32[2,128]{1,0:T(2,128)S(1)} %pad_maximum_fusion.3), channel_id=1, replica_groups=mesh['ctx'=64,'head'=4] {'head'}, use_global_device_ids=true, to_apply=%region_18.19 | all-reduce | flops 256 | bytes 2048 | tf_op jit(solution)/shard_map/psum | solution.py:169
  73.9 4.6 %collective-permute-start.5 = (bf16[8,128,128]{2,1,0:T(8,128)(2,1)S(1)}, bf16[8,128,128]{2,1,0:T(8,128)(2,1)S(1)}, u32[]{:S(2)}, u32[]{:S(2)}) collective-permute-start(bf16[8,128,128]{2,1,0:T(8,128)(2,1)S(1)} %get-tuple-element.82), channel_id=1, source_target_pairs={{4,0},{8,4},{12,8},{16,12},{20,16},{24,20},{28,24},{32,28},{36,32}... | collective-permute-start | bytes 786440 | tf_op jit(solution)/shard_map/ppermute | solution.py:15
  79.1 10.4 %collective-permute-done.5 = bf16[8,128,128]{2,1,0:T(8,128)(2,1)S(1)} collective-permute-done((bf16[8,128,128]{2,1,0:T(8,128)(2,1)S(1)}, bf16[8,128,128]{2,1,0:T(8,128)(2,1)S(1)}, u32[]{:S(2)}, u32[]{:S(2)}) %collective-permute-start.5) | collective-permute-done | bytes 262176 | tf_op jit(solution)/shard_map/ppermute | solution.py:15
  89.6 1.9 %collective-permute-start.8 = (bf16[8,128,128]{2,1,0:T(8,128)(2,1)S(1)}, bf16[8,128,128]{2,1,0:T(8,128)(2,1)S(1)}, u32[]{:S(2)}, u32[]{:S(2)}) collective-permute-start(bf16[8,128,128]{2,1,0:T(8,128)(2,1)S(1)} %get-tuple-element.45), channel_id=1, source_target_pairs={{8,0},{12,4},{16,8},{20,12},{24,16},{28,20},{32,24},{36,28},{40,32... | collective-permute-start | bytes 786440 | tf_op jit(solution)/shard_map/ppermute | solution.py:15
  91.6 0.7 fusion.29
  92.3 8.9 %collective-permute-done.8 = bf16[8,128,128]{2,1,0:T(8,128)(2,1)S(1)} collective-permute-done((bf16[8,128,128]{2,1,0:T(8,128)(2,1)S(1)}, bf16[8,128,128]{2,1,0:T(8,128)(2,1)S(1)}, u32[]{:S(2)}, u32[]{:S(2)}) %collective-permute-start.8) | collective-permute-done | bytes 262176 | tf_op jit(solution)/shard_map/ppermute | solution.py:15
  101.2 1.9 %collective-permute-start.9 = (bf16[8,128,128]{2,1,0:T(8,128)(2,1)S(1)}, bf16[8,128,128]{2,1,0:T(8,128)(2,1)S(1)}, u32[]{:S(2)}, u32[]{:S(2)}) collective-permute-start(bf16[8,128,128]{2,1,0:T(8,128)(2,1)S(1)} %fusion.55), channel_id=1, source_target_pairs={{16,0},{20,4},{24,8},{28,12},{32,16},{36,20},{40,24},{44,28},{48,3... | collective-permute-start | bytes 786440 | tf_op jit(solution)/shard_map/ppermute | solution.py:15
  103.4 10.7 %collective-permute-done.9 = bf16[8,128,128]{2,1,0:T(8,128)(2,1)S(1)} collective-permute-done((bf16[8,128,128]{2,1,0:T(8,128)(2,1)S(1)}, bf16[8,128,128]{2,1,0:T(8,128)(2,1)S(1)}, u32[]{:S(2)}, u32[]{:S(2)}) %collective-permute-start.9) | collective-permute-done | bytes 262176 | tf_op jit(solution)/shard_map/ppermute | solution.py:15
  114.3 1.9 %collective-permute-start.11 = (bf16[8,128,128]{2,1,0:T(8,128)(2,1)S(1)}, bf16[8,128,128]{2,1,0:T(8,128)(2,1)S(1)}, u32[]{:S(2)}, u32[]{:S(2)}) collective-permute-start(bf16[8,128,128]{2,1,0:T(8,128)(2,1)S(1)} %add_convert_fusion), channel_id=1, source_target_pairs={{36,0},{40,4},{44,8},{48,12},{52,16},{56,20},{60,24},{64,28},{68,3... | collective-permute-start | bytes 786440 | tf_op jit(solution)/shard_map/ppermute | solution.py:15
  116.2 2.2 %collective-permute-start.10 = (bf16[8,128,128]{2,1,0:T(8,128)(2,1)S(1)}, bf16[8,128,128]{2,1,0:T(8,128)(2,1)S(1)}, u32[]{:S(2)}, u32[]{:S(2)}) collective-permute-start(bf16[8,128,128]{2,1,0:T(8,128)(2,1)S(1)} %add_convert_fusion), channel_id=1, source_target_pairs={{4,0},{8,4},{12,8},{16,12},{20,16},{24,20},{28,24},{32,28},{36,32}... | collective-permute-start | bytes 786440 | tf_op jit(solution)/shard_map/ppermute | solution.py:15
  118.6 0.9 copy.204
  119.5 0.9 copy.205
  120.6 6.8 %collective-permute-done.11 = bf16[8,128,128]{2,1,0:T(8,128)(2,1)S(1)} collective-permute-done((bf16[8,128,128]{2,1,0:T(8,128)(2,1)S(1)}, bf16[8,128,128]{2,1,0:T(8,128)(2,1)S(1)}, u32[]{:S(2)}, u32[]{:S(2)}) %collective-permute-start.11) | collective-permute-done | bytes 262176 | tf_op jit(solution)/shard_map/ppermute | solution.py:15
  127.4 2.6 %collective-permute-done.10 = bf16[8,128,128]{2,1,0:T(8,128)(2,1)S(1)} collective-permute-done((bf16[8,128,128]{2,1,0:T(8,128)(2,1)S(1)}, bf16[8,128,128]{2,1,0:T(8,128)(2,1)S(1)}, u32[]{:S(2)}, u32[]{:S(2)}) %collective-permute-start.10) | collective-permute-done | bytes 262176 | tf_op jit(solution)/shard_map/ppermute | solution.py:15
  130.1 0.5 fusion.26
  130.5 1.3 fusion.31
  131.8 0.7 fusion.28
  132.5 1.3 fusion.35
  133.8 0.9 copy.206
  134.7 0.9 copy.207
  (87 shorter events, 9.9 us)
Async XLA Ops:
  1.8 8.8 %copy-start.8 = (s32[64]{0:T(128)S(1)}, s32[64]{0:T(128)}, u32[]{:S(2)}) copy-start(s32[64]{0:T(128)} %param.10) | copy-start | bytes 772
  1.8 29.5 %collective-permute-start.1 = (bf16[2,128,8,128]{3,1,2,0:T(8,128)(2,1)S(1)}, bf16[2,128,8,128]{3,1,2,0:T(8,128)(2,1)S(1)}, u32[]{:S(2)}, u32[]{:S(2)}) collective-permute-start(bf16[2,128,8,128]{3,1,2,0:T(8,128)(2,1)S(1)} %pad_maximum_fusion), channel_id=1, source_target_pairs={{0,8},{4,12},{8,16},{12,20},{16,24},{20,28},{24,32},{28,36},{32,40... | collective-permute-start | bytes 1572872 | tf_op jit(solution)/shard_map/ppermute | solution.py:15
  6.5 25.1 %collective-permute-start = (bf16[2,128,8,128]{3,1,2,0:T(8,128)(2,1)S(1)}, bf16[2,128,8,128]{3,1,2,0:T(8,128)(2,1)S(1)}, u32[]{:S(2)}, u32[]{:S(2)}) collective-permute-start(bf16[2,128,8,128]{3,1,2,0:T(8,128)(2,1)S(1)} %pad_maximum_fusion), channel_id=1, source_target_pairs={{0,4},{4,8},{8,12},{12,16},{16,20},{20,24},{24,28},{28,32},{32,36}... | collective-permute-start | bytes 1572872 | tf_op jit(solution)/shard_map/ppermute | solution.py:15
  10.5 20.5 %copy-start.3 = (bf16[128,8,128]{2,1,0:T(8,128)(2,1)S(1)}, bf16[128,8,128]{2,1,0:T(8,128)(2,1)}, u32[]{:S(2)}) copy-start(bf16[128,8,128]{2,1,0:T(8,128)(2,1)} %param.7) | copy-start | bytes 786436
  10.5 20.5 %copy-start.1 = (bf16[128,8,128]{2,1,0:T(8,128)(2,1)S(1)}, bf16[128,8,128]{2,1,0:T(8,128)(2,1)}, u32[]{:S(2)}) copy-start(bf16[128,8,128]{2,1,0:T(8,128)(2,1)} %param.6) | copy-start | bytes 786436
  32.0 1.0 copy-start
  33.2 1.0 copy-start.2
  35.1 9.3 %collective-permute-start.2 = (bf16[8,128,128]{2,1,0:T(8,128)(2,1)S(1)}, bf16[8,128,128]{2,1,0:T(8,128)(2,1)S(1)}, u32[]{:S(2)}, u32[]{:S(2)}) collective-permute-start(bf16[8,128,128]{2,1,0:T(8,128)(2,1)S(1)} %get-tuple-element.71), channel_id=1, source_target_pairs={{0,8},{4,12},{8,16},{12,20},{16,24},{20,28},{24,32},{28,36},{32,40... | collective-permute-start | bytes 786440 | tf_op jit(solution)/shard_map/ppermute | solution.py:15
  44.5 11.2 %collective-permute-start.3 = (bf16[8,128,128]{2,1,0:T(8,128)(2,1)S(1)}, bf16[8,128,128]{2,1,0:T(8,128)(2,1)S(1)}, u32[]{:S(2)}, u32[]{:S(2)}) collective-permute-start(bf16[8,128,128]{2,1,0:T(8,128)(2,1)S(1)} %fusion.54), channel_id=1, source_target_pairs={{0,16},{4,20},{8,24},{12,28},{16,32},{20,36},{24,40},{28,44},{32,4... | collective-permute-start | bytes 786440 | tf_op jit(solution)/shard_map/ppermute | solution.py:15
  55.9 10.5 %collective-permute-start.4 = (bf16[8,128,128]{2,1,0:T(8,128)(2,1)S(1)}, bf16[8,128,128]{2,1,0:T(8,128)(2,1)S(1)}, u32[]{:S(2)}, u32[]{:S(2)}) collective-permute-start(bf16[8,128,128]{2,1,0:T(8,128)(2,1)S(1)} %convert_element_type.228), channel_id=1, source_target_pairs={{0,32},{4,36},{8,40},{12,44},{16,48},{20,52},{24,56},{28,60},{32,6... | collective-permute-start | bytes 786440 | tf_op jit(solution)/shard_map/ppermute | solution.py:15
  59.6 29.9 %collective-permute-start.6 = (bf16[2,128,8,128]{3,1,2,0:T(8,128)(2,1)}, bf16[2,128,8,128]{3,1,2,0:T(8,128)(2,1)}, u32[]{:S(2)}, u32[]{:S(2)}) collective-permute-start(bf16[2,128,8,128]{3,1,2,0:T(8,128)(2,1)} %pad_maximum_fusion.1), channel_id=1, source_target_pairs={{4,0},{8,4},{12,8},{16,12},{20,16},{24,20},{28,24},{32,28},{36,32}... | collective-permute-start | bytes 1572872 | tf_op jit(solution)/shard_map/ppermute | solution.py:15
  62.7 26.8 %collective-permute-start.7 = (bf16[2,128,8,128]{3,1,2,0:T(8,128)(2,1)}, bf16[2,128,8,128]{3,1,2,0:T(8,128)(2,1)}, u32[]{:S(2)}, u32[]{:S(2)}) collective-permute-start(bf16[2,128,8,128]{3,1,2,0:T(8,128)(2,1)} %pad_maximum_fusion.2), channel_id=1, source_target_pairs={{8,0},{12,4},{16,8},{20,12},{24,16},{28,20},{32,24},{36,28},{40,32... | collective-permute-start | bytes 1572872 | tf_op jit(solution)/shard_map/ppermute | solution.py:15
  66.4 0.7 copy-start.5
  66.4 0.7 copy-start.7
  73.5 5.0 %copy-start.4 = (f32[128,8,128]{2,0,1:T(8,128)S(1)}, f32[128,8,128]{2,0,1:T(8,128)}, u32[]{:S(2)}) copy-start(f32[128,8,128]{2,0,1:T(8,128)} %fusion.14) | copy-start | bytes 1572868
  73.9 15.6 %collective-permute-start.5 = (bf16[8,128,128]{2,1,0:T(8,128)(2,1)S(1)}, bf16[8,128,128]{2,1,0:T(8,128)(2,1)S(1)}, u32[]{:S(2)}, u32[]{:S(2)}) collective-permute-start(bf16[8,128,128]{2,1,0:T(8,128)(2,1)S(1)} %get-tuple-element.82), channel_id=1, source_target_pairs={{4,0},{8,4},{12,8},{16,12},{20,16},{24,20},{28,24},{32,28},{36,32}... | collective-permute-start | bytes 786440 | tf_op jit(solution)/shard_map/ppermute | solution.py:15
  89.5 2.0 %copy-start.6 = (bf16[8,128,128]{2,1,0:T(8,128)(2,1)S(1)}, bf16[8,128,128]{2,1,0:T(8,128)(2,1)}, u32[]{:S(2)}) copy-start(bf16[8,128,128]{2,1,0:T(8,128)(2,1)} %copy-done.5) | copy-start | bytes 786436
  89.6 11.5 %collective-permute-start.8 = (bf16[8,128,128]{2,1,0:T(8,128)(2,1)S(1)}, bf16[8,128,128]{2,1,0:T(8,128)(2,1)S(1)}, u32[]{:S(2)}, u32[]{:S(2)}) collective-permute-start(bf16[8,128,128]{2,1,0:T(8,128)(2,1)S(1)} %get-tuple-element.45), channel_id=1, source_target_pairs={{8,0},{12,4},{16,8},{20,12},{24,16},{28,20},{32,24},{36,28},{40,32... | collective-permute-start | bytes 786440 | tf_op jit(solution)/shard_map/ppermute | solution.py:15
  101.2 12.9 %collective-permute-start.9 = (bf16[8,128,128]{2,1,0:T(8,128)(2,1)S(1)}, bf16[8,128,128]{2,1,0:T(8,128)(2,1)S(1)}, u32[]{:S(2)}, u32[]{:S(2)}) collective-permute-start(bf16[8,128,128]{2,1,0:T(8,128)(2,1)S(1)} %fusion.55), channel_id=1, source_target_pairs={{16,0},{20,4},{24,8},{28,12},{32,16},{36,20},{40,24},{44,28},{48,3... | collective-permute-start | bytes 786440 | tf_op jit(solution)/shard_map/ppermute | solution.py:15
  114.3 13.1 %collective-permute-start.11 = (bf16[8,128,128]{2,1,0:T(8,128)(2,1)S(1)}, bf16[8,128,128]{2,1,0:T(8,128)(2,1)S(1)}, u32[]{:S(2)}, u32[]{:S(2)}) collective-permute-start(bf16[8,128,128]{2,1,0:T(8,128)(2,1)S(1)} %add_convert_fusion), channel_id=1, source_target_pairs={{36,0},{40,4},{44,8},{48,12},{52,16},{56,20},{60,24},{64,28},{68,3... | collective-permute-start | bytes 786440 | tf_op jit(solution)/shard_map/ppermute | solution.py:15
  116.2 13.8 %collective-permute-start.10 = (bf16[8,128,128]{2,1,0:T(8,128)(2,1)S(1)}, bf16[8,128,128]{2,1,0:T(8,128)(2,1)S(1)}, u32[]{:S(2)}, u32[]{:S(2)}) collective-permute-start(bf16[8,128,128]{2,1,0:T(8,128)(2,1)S(1)} %add_convert_fusion), channel_id=1, source_target_pairs={{4,0},{8,4},{12,8},{16,12},{20,16},{24,20},{28,24},{32,28},{36,32}... | collective-permute-start | bytes 786440 | tf_op jit(solution)/shard_map/ppermute | solution.py:15
where the time goes:
time: 136 us
  waiting for transfers between devices  48.6 us (36%)
  starting transfers between devices  37.7 us (28%)
  matrix products  12.8 us (9%)
  local copies, waits for them, and re-layouts  12.4 us (9%)
  between operations  12 us (9%)
  other arithmetic  6.32 us (5%)
  blocking collectives  5.76 us (4%)
    ppermute x12, waiting for transfers between devices, from_behind(): return lax.ppermute(x, axis, pairs)  48.6 us
    ppermute x12, starting transfers between devices, from_behind(): return lax.ppermute(x, axis, pairs)  37.7 us
    dot_general x26, matrix products, narrow(): return jnp.einsum(form, left, right, preferred_element_type=jnp.float32)  10.5 us
    psum x1, blocking collectives, per_device(): lax.psum(jnp.stack([jnp.sum(linear_out * linear_out, axis=(1, 2)), jnp.su...  5.76 us
    unnamed x22, local copies, waits for them, and re-layouts  5.14 us
  transfers between devices with their start and end apart: 12, of which 7 were waited for; matrix products, arithmetic and copies ran while one was open for 15% of the time, Pallas kernels for 0%

commit v1 on v0

--- a/solution.py
+++ b/solution.py
@@ -166,14 +166,17 @@
         + wide("thd,hde->the", query_wide, incoming) * carried_prev[:, None, None]
     )
     weighted = cotangent.astype(jnp.float32) * gain[None]
-    squares, projection = lax.psum(
-        jnp.stack(
-            [
-                jnp.sum(linear_out * linear_out, axis=(1, 2)),
-                jnp.sum(weighted * linear_out, axis=(1, 2)),
-            ]
+    squares, projection = jnp.sum(
+        lax.all_gather(
+            jnp.stack(
+                [
+                    jnp.sum(linear_out * linear_out, axis=(1, 2)),
+                    jnp.sum(weighted * linear_out, axis=(1, 2)),
+                ]
+            ),
+            "head",
         ),
-        "head",
+        axis=0,
     )
     inverse = lax.rsqrt(squares / features + norm_eps)
     mixed = (linear_out * inverse[:, None, None] * gain[None] + soft_out).astype(jnp.bfloat16)

time: 136 us -> 136 us (level)
    psum x1 -> x0, blocking collectives: 5.76 us -> none  [per_device(): lax.psum(jnp.stack([jnp.sum(linear_out * linear_out, axis=(1, 2)), jnp.su...]
    all_gather x0 -> x1, blocking collectives: none -> 5 us  [per_device(): lax.all_gather(jnp.stack([jnp.sum(linear_out * linear_out, axis=(1, 2)),...]
where the time goes in v1:
time: 136 us
  waiting for transfers between devices  49.2 us (36%)
  starting transfers between devices  37.8 us (28%)
  matrix products  12.8 us (9%)
  local copies, waits for them, and re-layouts  12.4 us (9%)
  between operations  12 us (9%)
  other arithmetic  6.34 us (5%)
  blocking collectives  5 us (4%)
    ppermute x12, waiting for transfers between devices, from_behind(): return lax.ppermute(x, axis, pairs)  49.2 us
    ppermute x12, starting transfers between devices, from_behind(): return lax.ppermute(x, axis, pairs)  37.8 us
    dot_general x26, matrix products, narrow(): return jnp.einsum(form, left, right, preferred_element_type=jnp.float32)  10.5 us
    unnamed x22, local copies, waits for them, and re-layouts  5.14 us
    all_gather x1, blocking collectives, per_device(): lax.all_gather(jnp.stack([jnp.sum(linear_out * linear_out, axis=(1, 2)),...  5 us
  transfers between devices with their start and end apart: 12, of which 7 were waited for; matrix products, arithmetic and copies ran while one was open for 15% of the time, Pallas kernels for 0%

profile of v1, /device:TPU:127, one launch (start us, length us, event | category | flops | bytes accessed | tf_op | source)
XLA Modules:
  0.0 135.6 jit_solution(17215246734839516701)
XLA Ops:
  0.6 1.1 copy_bitcast_fusion
  1.8 4.7 %collective-permute-start.1 = (bf16[2,128,8,128]{3,1,2,0:T(8,128)(2,1)S(1)}, bf16[2,128,8,128]{3,1,2,0:T(8,128)(2,1)S(1)}, u32[]{:S(2)}, u32[]{:S(2)}) collective-permute-start(bf16[2,128,8,128]{3,1,2,0:T(8,128)(2,1)S(1)} %pad_maximum_fusion), channel_id=1, source_target_pairs={{0,8},{4,12},{8,16},{12,20},{16,24},{20,28},{24,32},{28,36},{32,40... | collective-permute-start | bytes 1572872 | tf_op jit(solution)/shard_map/ppermute | solution.py:15
  6.5 4.0 %collective-permute-start = (bf16[2,128,8,128]{3,1,2,0:T(8,128)(2,1)S(1)}, bf16[2,128,8,128]{3,1,2,0:T(8,128)(2,1)S(1)}, u32[]{:S(2)}, u32[]{:S(2)}) collective-permute-start(bf16[2,128,8,128]{3,1,2,0:T(8,128)(2,1)S(1)} %pad_maximum_fusion), channel_id=1, source_target_pairs={{0,4},{4,8},{8,12},{12,16},{16,20},{20,24},{24,28},{28,32},{32,36}... | collective-permute-start | bytes 1572872 | tf_op jit(solution)/shard_map/ppermute | solution.py:15
  10.9 0.6 fusion.111
  13.9 0.6 fusion.126
  14.4 0.6 fusion.121
  15.1 0.6 fusion.122
  15.7 0.6 fusion.123
  16.3 0.6 slice.87
  16.9 0.6 slice.94
  17.7 1.3 broadcast_compare_fusion.1
  19.1 0.6 fusion.124
  19.7 0.7 fusion.125
  20.3 0.6 fusion.120
  20.9 0.6 slice.92
  32.3 0.6 copy-done
  33.4 0.7 copy-done.2
  35.1 3.1 %collective-permute-start.2 = (bf16[8,128,128]{2,1,0:T(8,128)(2,1)S(1)}, bf16[8,128,128]{2,1,0:T(8,128)(2,1)S(1)}, u32[]{:S(2)}, u32[]{:S(2)}) collective-permute-start(bf16[8,128,128]{2,1,0:T(8,128)(2,1)S(1)} %get-tuple-element.75), channel_id=1, source_target_pairs={{0,8},{4,12},{8,16},{12,20},{16,24},{20,28},{24,32},{28,36},{32,40... | collective-permute-start | bytes 786440 | tf_op jit(solution)/shard_map/ppermute | solution.py:15
  40.1 0.9 pad_maximum_fusion.2
  41.3 3.2 %collective-permute-done.2 = bf16[8,128,128]{2,1,0:T(8,128)(2,1)S(1)} collective-permute-done((bf16[8,128,128]{2,1,0:T(8,128)(2,1)S(1)}, bf16[8,128,128]{2,1,0:T(8,128)(2,1)S(1)}, u32[]{:S(2)}, u32[]{:S(2)}) %collective-permute-start.2) | collective-permute-done | bytes 262176 | tf_op jit(solution)/shard_map/ppermute | solution.py:15
  44.5 4.0 %collective-permute-start.3 = (bf16[8,128,128]{2,1,0:T(8,128)(2,1)S(1)}, bf16[8,128,128]{2,1,0:T(8,128)(2,1)S(1)}, u32[]{:S(2)}, u32[]{:S(2)}) collective-permute-start(bf16[8,128,128]{2,1,0:T(8,128)(2,1)S(1)} %fusion.54), channel_id=1, source_target_pairs={{0,16},{4,20},{8,24},{12,28},{16,32},{20,36},{24,40},{28,44},{32,4... | collective-permute-start | bytes 786440 | tf_op jit(solution)/shard_map/ppermute | solution.py:15
  48.6 0.9 pad_maximum_fusion.1
  49.8 6.0 %collective-permute-done.3 = bf16[8,128,128]{2,1,0:T(8,128)(2,1)S(1)} collective-permute-done((bf16[8,128,128]{2,1,0:T(8,128)(2,1)S(1)}, bf16[8,128,128]{2,1,0:T(8,128)(2,1)S(1)}, u32[]{:S(2)}, u32[]{:S(2)}) %collective-permute-start.3) | collective-permute-done | bytes 262176 | tf_op jit(solution)/shard_map/ppermute | solution.py:15
  55.9 2.6 %collective-permute-start.4 = (bf16[8,128,128]{2,1,0:T(8,128)(2,1)S(1)}, bf16[8,128,128]{2,1,0:T(8,128)(2,1)S(1)}, u32[]{:S(2)}, u32[]{:S(2)}) collective-permute-start(bf16[8,128,128]{2,1,0:T(8,128)(2,1)S(1)} %convert_element_type.228), channel_id=1, source_target_pairs={{0,32},{4,36},{8,40},{12,44},{16,48},{20,52},{24,56},{28,60},{32,6... | collective-permute-start | bytes 786440 | tf_op jit(solution)/shard_map/ppermute | solution.py:15
  58.5 1.1 fusion.14
  59.6 3.1 %collective-permute-start.6 = (bf16[2,128,8,128]{3,1,2,0:T(8,128)(2,1)}, bf16[2,128,8,128]{3,1,2,0:T(8,128)(2,1)}, u32[]{:S(2)}, u32[]{:S(2)}) collective-permute-start(bf16[2,128,8,128]{3,1,2,0:T(8,128)(2,1)} %pad_maximum_fusion.1), channel_id=1, source_target_pairs={{4,0},{8,4},{12,8},{16,12},{20,16},{24,20},{28,24},{32,28},{36,32}... | collective-permute-start | bytes 1572872 | tf_op jit(solution)/shard_map/ppermute | solution.py:15
  62.7 3.6 %collective-permute-start.7 = (bf16[2,128,8,128]{3,1,2,0:T(8,128)(2,1)}, bf16[2,128,8,128]{3,1,2,0:T(8,128)(2,1)}, u32[]{:S(2)}, u32[]{:S(2)}) collective-permute-start(bf16[2,128,8,128]{3,1,2,0:T(8,128)(2,1)} %pad_maximum_fusion.2), channel_id=1, source_target_pairs={{8,0},{12,4},{16,8},{20,12},{24,16},{28,20},{32,24},{36,28},{40,32... | collective-permute-start | bytes 1572872 | tf_op jit(solution)/shard_map/ppermute | solution.py:15
  66.4 0.5 fusion.30
  67.5 5.0 %all-gather.1 = f32[4,2,128]{2,1,0:T(2,128)S(1)} all-gather(f32[1,2,128]{2,1,0:T(2,128)S(1)} %maximum_bitcast_fusion), channel_id=2, replica_groups=mesh['ctx'=64,'head'=4] {'head'}, dimensions={0}, use_global_device_ids=true | all-gather | bytes 5120 | tf_op jit(solution)/shard_map/all_gather | solution.py:170
  73.2 4.6 %collective-permute-start.5 = (bf16[8,128,128]{2,1,0:T(8,128)(2,1)S(1)}, bf16[8,128,128]{2,1,0:T(8,128)(2,1)S(1)}, u32[]{:S(2)}, u32[]{:S(2)}) collective-permute-start(bf16[8,128,128]{2,1,0:T(8,128)(2,1)S(1)} %get-tuple-element.86), channel_id=1, source_target_pairs={{4,0},{8,4},{12,8},{16,12},{20,16},{24,20},{28,24},{32,28},{36,32}... | collective-permute-start | bytes 786440 | tf_op jit(solution)/shard_map/ppermute | solution.py:15
  78.4 11.0 %collective-permute-done.5 = bf16[8,128,128]{2,1,0:T(8,128)(2,1)S(1)} collective-permute-done((bf16[8,128,128]{2,1,0:T(8,128)(2,1)S(1)}, bf16[8,128,128]{2,1,0:T(8,128)(2,1)S(1)}, u32[]{:S(2)}, u32[]{:S(2)}) %collective-permute-start.5) | collective-permute-done | bytes 262176 | tf_op jit(solution)/shard_map/ppermute | solution.py:15
  89.5 1.9 %collective-permute-start.8 = (bf16[8,128,128]{2,1,0:T(8,128)(2,1)S(1)}, bf16[8,128,128]{2,1,0:T(8,128)(2,1)S(1)}, u32[]{:S(2)}, u32[]{:S(2)}) collective-permute-start(bf16[8,128,128]{2,1,0:T(8,128)(2,1)S(1)} %get-tuple-element.49), channel_id=1, source_target_pairs={{8,0},{12,4},{16,8},{20,12},{24,16},{28,20},{32,24},{36,28},{40,32... | collective-permute-start | bytes 786440 | tf_op jit(solution)/shard_map/ppermute | solution.py:15
  91.5 0.7 fusion.29
  92.2 9.0 %collective-permute-done.8 = bf16[8,128,128]{2,1,0:T(8,128)(2,1)S(1)} collective-permute-done((bf16[8,128,128]{2,1,0:T(8,128)(2,1)S(1)}, bf16[8,128,128]{2,1,0:T(8,128)(2,1)S(1)}, u32[]{:S(2)}, u32[]{:S(2)}) %collective-permute-start.8) | collective-permute-done | bytes 262176 | tf_op jit(solution)/shard_map/ppermute | solution.py:15
  101.2 1.9 %collective-permute-start.9 = (bf16[8,128,128]{2,1,0:T(8,128)(2,1)S(1)}, bf16[8,128,128]{2,1,0:T(8,128)(2,1)S(1)}, u32[]{:S(2)}, u32[]{:S(2)}) collective-permute-start(bf16[8,128,128]{2,1,0:T(8,128)(2,1)S(1)} %fusion.55), channel_id=1, source_target_pairs={{16,0},{20,4},{24,8},{28,12},{32,16},{36,20},{40,24},{44,28},{48,3... | collective-permute-start | bytes 786440 | tf_op jit(solution)/shard_map/ppermute | solution.py:15
  103.4 10.8 %collective-permute-done.9 = bf16[8,128,128]{2,1,0:T(8,128)(2,1)S(1)} collective-permute-done((bf16[8,128,128]{2,1,0:T(8,128)(2,1)S(1)}, bf16[8,128,128]{2,1,0:T(8,128)(2,1)S(1)}, u32[]{:S(2)}, u32[]{:S(2)}) %collective-permute-start.9) | collective-permute-done | bytes 262176 | tf_op jit(solution)/shard_map/ppermute | solution.py:15
  114.4 1.9 %collective-permute-start.11 = (bf16[8,128,128]{2,1,0:T(8,128)(2,1)S(1)}, bf16[8,128,128]{2,1,0:T(8,128)(2,1)S(1)}, u32[]{:S(2)}, u32[]{:S(2)}) collective-permute-start(bf16[8,128,128]{2,1,0:T(8,128)(2,1)S(1)} %add_convert_fusion), channel_id=1, source_target_pairs={{36,0},{40,4},{44,8},{48,12},{52,16},{56,20},{60,24},{64,28},{68,3... | collective-permute-start | bytes 786440 | tf_op jit(solution)/shard_map/ppermute | solution.py:15
  116.3 2.3 %collective-permute-start.10 = (bf16[8,128,128]{2,1,0:T(8,128)(2,1)S(1)}, bf16[8,128,128]{2,1,0:T(8,128)(2,1)S(1)}, u32[]{:S(2)}, u32[]{:S(2)}) collective-permute-start(bf16[8,128,128]{2,1,0:T(8,128)(2,1)S(1)} %add_convert_fusion), channel_id=1, source_target_pairs={{4,0},{8,4},{12,8},{16,12},{20,16},{24,20},{28,24},{32,28},{36,32}... | collective-permute-start | bytes 786440 | tf_op jit(solution)/shard_map/ppermute | solution.py:15
  118.8 0.9 copy.270
  119.7 0.9 copy.271
  120.8 6.5 %collective-permute-done.11 = bf16[8,128,128]{2,1,0:T(8,128)(2,1)S(1)} collective-permute-done((bf16[8,128,128]{2,1,0:T(8,128)(2,1)S(1)}, bf16[8,128,128]{2,1,0:T(8,128)(2,1)S(1)}, u32[]{:S(2)}, u32[]{:S(2)}) %collective-permute-start.11) | collective-permute-done | bytes 262176 | tf_op jit(solution)/shard_map/ppermute | solution.py:15
  127.3 2.7 %collective-permute-done.10 = bf16[8,128,128]{2,1,0:T(8,128)(2,1)S(1)} collective-permute-done((bf16[8,128,128]{2,1,0:T(8,128)(2,1)S(1)}, bf16[8,128,128]{2,1,0:T(8,128)(2,1)S(1)}, u32[]{:S(2)}, u32[]{:S(2)}) %collective-permute-start.10) | collective-permute-done | bytes 262176 | tf_op jit(solution)/shard_map/ppermute | solution.py:15
  130.1 0.5 fusion.26
  130.5 1.3 fusion.31
  131.8 0.7 fusion.28
  132.5 1.3 fusion.35
  133.9 0.9 copy.272
  134.7 0.9 copy.273
  (88 shorter events, 9.9 us)
Async XLA Ops:
  1.8 8.8 %copy-start.8 = (s32[64]{0:T(128)S(1)}, s32[64]{0:T(128)}, u32[]{:S(2)}) copy-start(s32[64]{0:T(128)} %param.10) | copy-start | bytes 772
  1.8 29.5 %collective-permute-start.1 = (bf16[2,128,8,128]{3,1,2,0:T(8,128)(2,1)S(1)}, bf16[2,128,8,128]{3,1,2,0:T(8,128)(2,1)S(1)}, u32[]{:S(2)}, u32[]{:S(2)}) collective-permute-start(bf16[2,128,8,128]{3,1,2,0:T(8,128)(2,1)S(1)} %pad_maximum_fusion), channel_id=1, source_target_pairs={{0,8},{4,12},{8,16},{12,20},{16,24},{20,28},{24,32},{28,36},{32,40... | collective-permute-start | bytes 1572872 | tf_op jit(solution)/shard_map/ppermute | solution.py:15
  6.5 25.1 %collective-permute-start = (bf16[2,128,8,128]{3,1,2,0:T(8,128)(2,1)S(1)}, bf16[2,128,8,128]{3,1,2,0:T(8,128)(2,1)S(1)}, u32[]{:S(2)}, u32[]{:S(2)}) collective-permute-start(bf16[2,128,8,128]{3,1,2,0:T(8,128)(2,1)S(1)} %pad_maximum_fusion), channel_id=1, source_target_pairs={{0,4},{4,8},{8,12},{12,16},{16,20},{20,24},{24,28},{28,32},{32,36}... | collective-permute-start | bytes 1572872 | tf_op jit(solution)/shard_map/ppermute | solution.py:15
  10.5 20.5 %copy-start.3 = (bf16[128,8,128]{2,1,0:T(8,128)(2,1)S(1)}, bf16[128,8,128]{2,1,0:T(8,128)(2,1)}, u32[]{:S(2)}) copy-start(bf16[128,8,128]{2,1,0:T(8,128)(2,1)} %param.7) | copy-start | bytes 786436
  10.5 20.5 %copy-start.1 = (bf16[128,8,128]{2,1,0:T(8,128)(2,1)S(1)}, bf16[128,8,128]{2,1,0:T(8,128)(2,1)}, u32[]{:S(2)}) copy-start(bf16[128,8,128]{2,1,0:T(8,128)(2,1)} %param.6) | copy-start | bytes 786436
  32.0 1.0 copy-start
  33.2 1.0 copy-start.2
  35.1 9.3 %collective-permute-start.2 = (bf16[8,128,128]{2,1,0:T(8,128)(2,1)S(1)}, bf16[8,128,128]{2,1,0:T(8,128)(2,1)S(1)}, u32[]{:S(2)}, u32[]{:S(2)}) collective-permute-start(bf16[8,128,128]{2,1,0:T(8,128)(2,1)S(1)} %get-tuple-element.75), channel_id=1, source_target_pairs={{0,8},{4,12},{8,16},{12,20},{16,24},{20,28},{24,32},{28,36},{32,40... | collective-permute-start | bytes 786440 | tf_op jit(solution)/shard_map/ppermute | solution.py:15
  44.5 11.2 %collective-permute-start.3 = (bf16[8,128,128]{2,1,0:T(8,128)(2,1)S(1)}, bf16[8,128,128]{2,1,0:T(8,128)(2,1)S(1)}, u32[]{:S(2)}, u32[]{:S(2)}) collective-permute-start(bf16[8,128,128]{2,1,0:T(8,128)(2,1)S(1)} %fusion.54), channel_id=1, source_target_pairs={{0,16},{4,20},{8,24},{12,28},{16,32},{20,36},{24,40},{28,44},{32,4... | collective-permute-start | bytes 786440 | tf_op jit(solution)/shard_map/ppermute | solution.py:15
  55.9 10.5 %collective-permute-start.4 = (bf16[8,128,128]{2,1,0:T(8,128)(2,1)S(1)}, bf16[8,128,128]{2,1,0:T(8,128)(2,1)S(1)}, u32[]{:S(2)}, u32[]{:S(2)}) collective-permute-start(bf16[8,128,128]{2,1,0:T(8,128)(2,1)S(1)} %convert_element_type.228), channel_id=1, source_target_pairs={{0,32},{4,36},{8,40},{12,44},{16,48},{20,52},{24,56},{28,60},{32,6... | collective-permute-start | bytes 786440 | tf_op jit(solution)/shard_map/ppermute | solution.py:15
  59.6 29.8 %collective-permute-start.6 = (bf16[2,128,8,128]{3,1,2,0:T(8,128)(2,1)}, bf16[2,128,8,128]{3,1,2,0:T(8,128)(2,1)}, u32[]{:S(2)}, u32[]{:S(2)}) collective-permute-start(bf16[2,128,8,128]{3,1,2,0:T(8,128)(2,1)} %pad_maximum_fusion.1), channel_id=1, source_target_pairs={{4,0},{8,4},{12,8},{16,12},{20,16},{24,20},{28,24},{32,28},{36,32}... | collective-permute-start | bytes 1572872 | tf_op jit(solution)/shard_map/ppermute | solution.py:15
  62.7 26.7 %collective-permute-start.7 = (bf16[2,128,8,128]{3,1,2,0:T(8,128)(2,1)}, bf16[2,128,8,128]{3,1,2,0:T(8,128)(2,1)}, u32[]{:S(2)}, u32[]{:S(2)}) collective-permute-start(bf16[2,128,8,128]{3,1,2,0:T(8,128)(2,1)} %pad_maximum_fusion.2), channel_id=1, source_target_pairs={{8,0},{12,4},{16,8},{20,12},{24,16},{28,20},{32,24},{36,28},{40,32... | collective-permute-start | bytes 1572872 | tf_op jit(solution)/shard_map/ppermute | solution.py:15
  66.4 0.7 copy-start.5
  66.4 0.7 copy-start.7
  72.8 5.0 %copy-start.4 = (f32[128,8,128]{2,0,1:T(8,128)S(1)}, f32[128,8,128]{2,0,1:T(8,128)}, u32[]{:S(2)}) copy-start(f32[128,8,128]{2,0,1:T(8,128)} %fusion.14) | copy-start | bytes 1572868
  73.2 16.2 %collective-permute-start.5 = (bf16[8,128,128]{2,1,0:T(8,128)(2,1)S(1)}, bf16[8,128,128]{2,1,0:T(8,128)(2,1)S(1)}, u32[]{:S(2)}, u32[]{:S(2)}) collective-permute-start(bf16[8,128,128]{2,1,0:T(8,128)(2,1)S(1)} %get-tuple-element.86), channel_id=1, source_target_pairs={{4,0},{8,4},{12,8},{16,12},{20,16},{24,20},{28,24},{32,28},{36,32}... | collective-permute-start | bytes 786440 | tf_op jit(solution)/shard_map/ppermute | solution.py:15
  89.4 2.0 %copy-start.6 = (bf16[8,128,128]{2,1,0:T(8,128)(2,1)S(1)}, bf16[8,128,128]{2,1,0:T(8,128)(2,1)}, u32[]{:S(2)}) copy-start(bf16[8,128,128]{2,1,0:T(8,128)(2,1)} %copy-done.5) | copy-start | bytes 786436
  89.5 11.6 %collective-permute-start.8 = (bf16[8,128,128]{2,1,0:T(8,128)(2,1)S(1)}, bf16[8,128,128]{2,1,0:T(8,128)(2,1)S(1)}, u32[]{:S(2)}, u32[]{:S(2)}) collective-permute-start(bf16[8,128,128]{2,1,0:T(8,128)(2,1)S(1)} %get-tuple-element.49), channel_id=1, source_target_pairs={{8,0},{12,4},{16,8},{20,12},{24,16},{28,20},{32,24},{36,28},{40,32... | collective-permute-start | bytes 786440 | tf_op jit(solution)/shard_map/ppermute | solution.py:15
  101.2 13.1 %collective-permute-start.9 = (bf16[8,128,128]{2,1,0:T(8,128)(2,1)S(1)}, bf16[8,128,128]{2,1,0:T(8,128)(2,1)S(1)}, u32[]{:S(2)}, u32[]{:S(2)}) collective-permute-start(bf16[8,128,128]{2,1,0:T(8,128)(2,1)S(1)} %fusion.55), channel_id=1, source_target_pairs={{16,0},{20,4},{24,8},{28,12},{32,16},{36,20},{40,24},{44,28},{48,3... | collective-permute-start | bytes 786440 | tf_op jit(solution)/shard_map/ppermute | solution.py:15
  114.4 12.9 %collective-permute-start.11 = (bf16[8,128,128]{2,1,0:T(8,128)(2,1)S(1)}, bf16[8,128,128]{2,1,0:T(8,128)(2,1)S(1)}, u32[]{:S(2)}, u32[]{:S(2)}) collective-permute-start(bf16[8,128,128]{2,1,0:T(8,128)(2,1)S(1)} %add_convert_fusion), channel_id=1, source_target_pairs={{36,0},{40,4},{44,8},{48,12},{52,16},{56,20},{60,24},{64,28},{68,3... | collective-permute-start | bytes 786440 | tf_op jit(solution)/shard_map/ppermute | solution.py:15
  116.3 13.7 %collective-permute-start.10 = (bf16[8,128,128]{2,1,0:T(8,128)(2,1)S(1)}, bf16[8,128,128]{2,1,0:T(8,128)(2,1)S(1)}, u32[]{:S(2)}, u32[]{:S(2)}) collective-permute-start(bf16[8,128,128]{2,1,0:T(8,128)(2,1)S(1)} %add_convert_fusion), channel_id=1, source_target_pairs={{4,0},{8,4},{12,8},{16,12},{20,16},{24,20},{28,24},{32,28},{36,32}... | collective-permute-start | bytes 786440 | tf_op jit(solution)/shard_map/ppermute | solution.py:15
